TPU v7x, 512 devices: a whole 4x8x8 slice. The times are simulated.
512 devices in a mesh: ctx: 128 (over z_hi, x, y), head: 4 (over z_lo, core).
Axes of the slice: x: 4, y: 8, z: 8 (z_hi: 4, z_lo: 2; z = z_hi * 2 + z_lo), core: 2. Of those that a mesh axis runs over, the one named last changes fastest.
Arguments:
- queries: bfloat16 [32768, 4096], P(('ctx', 'head')), may hold values from -200 to 200
- normed_key_state: bfloat16 [32768, 2048], P(('ctx', 'head')), may hold values from -5 to 5
- value_state_rows: bfloat16 [32768, 2048], P(('ctx', 'head')), may hold values from -6 to 6
- output_gradient: bfloat16 [32768, 4096], P(('ctx', 'head')), may hold values from -6 to 6
- doc_start: int32 [32768], P('ctx'), may hold values from 0 to 32767, as said below
Outputs:
- grad_queries: bfloat16 [32768, 4096], P(('ctx', 'head'))
- key_gradient: bfloat16 [32768, 2048], P(('ctx', 'head'))
- value_gradient: bfloat16 [32768, 2048], P(('ctx', 'head'))
Inputs may be any that keep to these rules, and one draw needn't show every extreme that they name: doc_start[t] is the first position of the document that holds token t: doc_start[0] = 0, each doc_start[t] equals t or doc_start[t - 1], and the last token, position 32767, begins a document of its own.
All inputs are finite; a program needn't handle non-finite values.
Results may differ from a plain program's by a relative error of at most 0.007.
Values may be sent and summed in bfloat16 or wider, within the bound.
No kernel may reach another device: no remote copies, remote signals or barrier semaphores. Data moves between devices by JAX's collectives and lax.ppermute only.
A program may use at most 64 MiB of HBM per device.

v0:
```python
import jax
import jax.numpy as jnp
from jax import lax
from jax.sharding import PartitionSpec as P

QUERY_HEADS = 32
KEY_VALUE_HEADS = 16
HEAD_SIZE = 128
WINDOW = 512
SPAN = 2
CHUNKS = 2
CHAIN = False
score_scale = 168.0 ** (-0.5)


def passed_along(block, axis, distance):
    devices = range(lax.axis_size(axis))
    route = [(i - distance, i) for i in devices if i - distance in devices]
    return lax.ppermute(block, axis, route)


def pair_scores(query_heads, key_block):
    return score_scale * jnp.einsum(
        "tgjd,kgd->gjtk", query_heads, key_block, preferred_element_type=jnp.float32
    )


def attend_chunk(kv_in, qg_in, doc_start):
    kv_all = lax.all_to_all(kv_in, "head", split_axis=1, concat_axis=0, tiled=True)
    tok_rows = kv_all.shape[0]
    kv_cols = kv_all.shape[-1]
    kv_groups = kv_cols // HEAD_SIZE
    group_share = QUERY_HEADS // KEY_VALUE_HEADS
    kv_local = jnp.moveaxis(kv_all[:, 0], 1, 0)
    kv_blocks = [kv_local]
    for distance in range(1, SPAN + 1):
        if CHAIN:
            kv_blocks.append(passed_along(kv_blocks[-1], "ctx", 1))
        else:
            kv_blocks.append(passed_along(kv_local, "ctx", distance))
    qg_all = lax.all_to_all(qg_in, "head", split_axis=1, concat_axis=0, tiled=True)
    query_heads = qg_all[:, 0, 0].reshape(tok_rows, kv_groups, group_share, HEAD_SIZE)
    grad_heads = qg_all[:, 0, 1].reshape(tok_rows, kv_groups, group_share, HEAD_SIZE)
    shard_index = lax.axis_index("ctx")
    local_iota = jnp.arange(tok_rows, dtype=jnp.int32)
    query_pos = shard_index * tok_rows + local_iota

    def visible(distance):
        key_pos = (shard_index - distance) * tok_rows + local_iota
        return (
            (key_pos[None, :] >= doc_start[:, None])
            & (key_pos[None, :] <= query_pos[:, None])
            & (query_pos[:, None] - key_pos[None, :] < WINDOW)
        )

    def unpack(kv_block):
        return (
            kv_block[0].reshape(tok_rows, kv_groups, HEAD_SIZE),
            kv_block[1].reshape(tok_rows, kv_groups, HEAD_SIZE),
        )

    masks = [visible(distance) for distance in range(SPAN + 1)]
    stat_shape = (kv_groups, group_share, tok_rows)
    running = (
        jnp.full(stat_shape, -jnp.inf, jnp.float32),
        jnp.zeros(stat_shape, jnp.float32),
        jnp.zeros(stat_shape, jnp.float32),
    )
    for distance in range(SPAN + 1):
        gather_key_block, gather_value_block = unpack(kv_blocks[distance])
        gather_masked = jnp.where(
            masks[distance], pair_scores(query_heads, gather_key_block), -jnp.inf
        )
        gather_dprob = jnp.einsum(
            "tgjd,kgd->gjtk", grad_heads, gather_value_block, preferred_element_type=jnp.float32
        )
        new_max = jnp.maximum(running[0], jnp.max(gather_masked, axis=-1))
        factor = jnp.exp(running[0] - new_max)
        weights = jnp.exp(gather_masked - new_max[..., None])
        running = (
            new_max,
            running[1] * factor + jnp.sum(weights, axis=-1),
            running[2] * factor + jnp.sum(weights * gather_dprob, axis=-1),
        )
    log_total = running[0] + jnp.log(running[1])
    delta = running[2] / running[1]
    query_total = jnp.zeros((tok_rows, kv_groups, group_share, HEAD_SIZE), jnp.float32)
    kv_parts = {}
    for distance in reversed(range(SPAN + 1)):
        key_block, value_block = unpack(kv_blocks[distance])
        masked = jnp.where(masks[distance], pair_scores(query_heads, key_block), -jnp.inf)
        prob = jnp.exp(masked - log_total[..., None])
        dprob = jnp.einsum(
            "tgjd,kgd->gjtk", grad_heads, value_block, preferred_element_type=jnp.float32
        )
        dscore = (prob * (dprob - delta[..., None])).astype(jnp.bfloat16)
        prob_half = prob.astype(jnp.bfloat16)
        query_part = score_scale * jnp.einsum(
            "gjtk,kgd->tgjd", dscore, key_block, preferred_element_type=jnp.float32
        )
        key_part = score_scale * jnp.einsum(
            "gjtk,tgjd->kgd", dscore, query_heads, preferred_element_type=jnp.float32
        )
        value_part = jnp.einsum(
            "gjtk,tgjd->kgd", prob_half, grad_heads, preferred_element_type=jnp.float32
        )
        query_total = query_total + query_part
        kv_parts[distance] = jnp.stack([key_part, value_part]).reshape(2, tok_rows, kv_cols)
    if CHAIN:
        carried = passed_along(kv_parts[2].astype(jnp.bfloat16), "ctx", -1)
        carried = passed_along((kv_parts[1] + carried).astype(jnp.bfloat16), "ctx", -1)
        kv_total = kv_parts[0] + carried
    else:
        kv_total = kv_parts[0]
        for distance in range(1, SPAN + 1):
            kv_total = kv_total + passed_along(
                kv_parts[distance].astype(jnp.bfloat16), "ctx", -distance
            )
    grad_query_loc = query_total.reshape(tok_rows, 1, kv_groups * group_share * HEAD_SIZE)
    grad_q = lax.all_to_all(
        grad_query_loc.astype(jnp.bfloat16), "head", split_axis=0, concat_axis=1, tiled=True
    )
    kv_out = jnp.moveaxis(kv_total.astype(jnp.bfloat16), 0, 1)[:, None]
    kv_back = lax.all_to_all(kv_out, "head", split_axis=0, concat_axis=1, tiled=True)
    return (grad_q, kv_back)


def local(queries, normed_key_state, value_state_rows, output_gradient, doc_start):
    heads_ax = lax.axis_size("head")
    rows_in = queries.shape[0]
    kv_cols = normed_key_state.shape[1] // (heads_ax * CHUNKS)
    q_cols = queries.shape[1] // (heads_ax * CHUNKS)
    keys = normed_key_state.reshape(rows_in, heads_ax, CHUNKS, kv_cols)
    values = value_state_rows.reshape(rows_in, heads_ax, CHUNKS, kv_cols)
    qs = queries.reshape(rows_in, heads_ax, CHUNKS, q_cols)
    gs = output_gradient.reshape(rows_in, heads_ax, CHUNKS, q_cols)
    dq_parts, dkv_parts = ([], [])
    for chunk in range(CHUNKS):
        kv_in = jnp.stack([keys[:, :, chunk], values[:, :, chunk]], axis=2)
        qg_in = jnp.stack([qs[:, :, chunk], gs[:, :, chunk]], axis=2)
        dq, dkv = attend_chunk(kv_in, qg_in, doc_start)
        dq_parts.append(dq)
        dkv_parts.append(dkv)
    grad_q = jnp.stack(dq_parts, axis=2).reshape(rows_in, heads_ax * CHUNKS * q_cols)
    dkv = jnp.stack(dkv_parts, axis=3)
    grad_k = dkv[:, :, 0].reshape(rows_in, heads_ax * CHUNKS * kv_cols)
    grad_v = dkv[:, :, 1].reshape(rows_in, heads_ax * CHUNKS * kv_cols)
    return (grad_q, grad_k, grad_v)


def solution(mesh):
    placed = (
        P(("ctx", "head"), None),
        P(("ctx", "head"), None),
        P(("ctx", "head"), None),
        P(("ctx", "head"), None),
        P("ctx"),
    )
    return jax.shard_map(
        local,
        mesh=mesh,
        in_specs=placed,
        out_specs=(P(("ctx", "head"), None), P(("ctx", "head"), None), P(("ctx", "head"), None)),
        check_vma=False,
    )
```

profile of v0, /device:TPU:184, one launch (start us, length us, event | category | flops | bytes accessed | tf_op | source)
XLA Modules:
  0.0 210.7 jit_solution(13500736151918691449)
XLA Ops:
  0.6 1.2 reshape.236
  4.3 3.6 %all-to-all-start = ((bf16[64,4,2,256]{3,2,0,1:T(2,128)(2,1)}), bf16[64,4,2,256]{3,2,0,1:T(2,128)(2,1)S(1)}, u32[]{:S(2)}, u32[]{:S(2)}) async-start(bf16[64,4,2,256]{3,2,0,1:T(2,128)(2,1)} %copy.203), calls=%async_computation | async-start | bytes 524288 | tf_op jit(solution)/shard_map/all_to_all | solution.py:29
  9.3 1.5 fusion.71
  10.8 1.2 pad_maximum_fusion
  12.0 1.2 pad_maximum_fusion.1
  13.3 1.2 copy.206
  17.1 3.4 %all-to-all-start.3 = ((bf16[64,4,2,256]{3,2,0,1:T(2,128)(2,1)}), bf16[64,4,2,256]{3,2,0,1:T(2,128)(2,1)S(1)}, u32[]{:S(2)}, u32[]{:S(2)}) async-start(bf16[64,4,2,256]{3,2,0,1:T(2,128)(2,1)} %copy.231), calls=%async_computation.3 | async-start | bytes 524288 | tf_op jit(solution)/shard_map/all_to_all | solution.py:29
  22.1 3.6 %collective-permute-start = (bf16[2,256,256]{2,1,0:T(8,128)(2,1)S(1)}, bf16[2,256,256]{2,1,0:T(8,128)(2,1)S(1)}, u32[]{:S(2)}, u32[]{:S(2)}) collective-permute-start(bf16[2,256,256]{2,1,0:T(8,128)(2,1)S(1)} %bitcast.375), channel_id=1, source_target_pairs={{0,8},{4,12},{8,16},{12,20},{16,24},{20,28},{24,32},{28,36},{32,40... | collective-permute-start | bytes 786440 | tf_op jit(solution)/shard_map/ppermute | solution.py:19
  25.8 3.5 %collective-permute-start.1 = (bf16[2,256,256]{2,1,0:T(8,128)(2,1)S(1)}, bf16[2,256,256]{2,1,0:T(8,128)(2,1)S(1)}, u32[]{:S(2)}, u32[]{:S(2)}) collective-permute-start(bf16[2,256,256]{2,1,0:T(8,128)(2,1)S(1)} %bitcast.377), channel_id=1, source_target_pairs={{0,4},{4,8},{8,12},{12,16},{16,20},{20,24},{24,28},{28,32},{32,36}... | collective-permute-start | bytes 786440 | tf_op jit(solution)/shard_map/ppermute | solution.py:19
  29.3 3.5 %all-to-all-start.1 = ((bf16[64,4,2,512]{3,2,0,1:T(2,128)(2,1)}), bf16[64,4,2,512]{3,2,0,1:T(2,128)(2,1)S(1)}, u32[]{:S(2)}, u32[]{:S(2)}) async-start(bf16[64,4,2,512]{3,2,0,1:T(2,128)(2,1)} %copy.206), calls=%async_computation.1 | async-start | bytes 1048576 | tf_op jit(solution)/shard_map/all_to_all | solution.py:41
  32.8 3.5 %collective-permute-start.3 = (bf16[2,256,256]{2,1,0:T(8,128)(2,1)S(1)}, bf16[2,256,256]{2,1,0:T(8,128)(2,1)S(1)}, u32[]{:S(2)}, u32[]{:S(2)}) collective-permute-start(bf16[2,256,256]{2,1,0:T(8,128)(2,1)S(1)} %bitcast.373), channel_id=1, source_target_pairs={{0,4},{4,8},{8,12},{12,16},{16,20},{20,24},{24,28},{28,32},{32,36}... | collective-permute-start | bytes 786440 | tf_op jit(solution)/shard_map/ppermute | solution.py:19
  36.3 4.8 %collective-permute-start.2 = (bf16[2,256,256]{2,1,0:T(8,128)(2,1)S(1)}, bf16[2,256,256]{2,1,0:T(8,128)(2,1)S(1)}, u32[]{:S(2)}, u32[]{:S(2)}) collective-permute-start(bf16[2,256,256]{2,1,0:T(8,128)(2,1)S(1)} %bitcast.374), channel_id=1, source_target_pairs={{0,8},{4,12},{8,16},{12,20},{16,24},{20,28},{24,32},{28,36},{32,40... | collective-permute-start | bytes 786440 | tf_op jit(solution)/shard_map/ppermute | solution.py:19
  42.9 1.6 collective-permute-done.1
  47.0 3.4 %collective-permute-done.3 = bf16[2,256,256]{2,1,0:T(8,128)(2,1)S(1)} collective-permute-done((bf16[2,256,256]{2,1,0:T(8,128)(2,1)S(1)}, bf16[2,256,256]{2,1,0:T(8,128)(2,1)S(1)}, u32[]{:S(2)}, u32[]{:S(2)}) %collective-permute-start.3) | collective-permute-done | bytes 262176 | tf_op jit(solution)/shard_map/ppermute | solution.py:19
  51.1 10.6 %collective-permute-done.2 = bf16[2,256,256]{2,1,0:T(8,128)(2,1)S(1)} collective-permute-done((bf16[2,256,256]{2,1,0:T(8,128)(2,1)S(1)}, bf16[2,256,256]{2,1,0:T(8,128)(2,1)S(1)}, u32[]{:S(2)}, u32[]{:S(2)}) %collective-permute-start.2) | collective-permute-done | bytes 262176 | tf_op jit(solution)/shard_map/ppermute | solution.py:19
  64.0 3.7 %all-to-all-start.4 = ((bf16[64,4,2,512]{3,2,0,1:T(2,128)(2,1)}), bf16[64,4,2,512]{3,2,0,1:T(2,128)(2,1)S(1)}, u32[]{:S(2)}, u32[]{:S(2)}) async-start(bf16[64,4,2,512]{3,2,0,1:T(2,128)(2,1)} %copy.234), calls=%async_computation.4 | async-start | bytes 1048576 | tf_op jit(solution)/shard_map/all_to_all | solution.py:41
  70.8 1.9 multiply_reduce_fusion.5
  72.7 1.9 multiply_reduce_fusion.4
  74.6 1.9 multiply_reduce_fusion.3
  81.1 1.2 fusion.83
  82.4 1.3 fusion.84
  83.8 1.9 fusion.82
  85.7 1.8 copy.246
  88.2 1.5 multiply_reduce_fusion.2
  94.1 1.4 multiply_convert_fusion.5
  103.5 1.3 pad_maximum_fusion.6
  104.8 2.0 collective-permute-start.4
  110.0 1.3 pad_maximum_fusion.7
  111.3 6.5 %collective-permute-start.5 = (bf16[2,256,256]{2,0,1:T(2,128)(2,1)}, bf16[2,256,256]{2,0,1:T(2,128)(2,1)}, u32[]{:S(2)}, u32[]{:S(2)}) collective-permute-start(bf16[2,256,256]{2,0,1:T(2,128)(2,1)} %pad_maximum_fusion.7), channel_id=1, source_target_pairs={{8,0},{12,4},{16,8},{20,12},{24,16},{28,20},{32,24},{36,28},{40,32... | collective-permute-start | bytes 786440 | tf_op jit(solution)/shard_map/ppermute | solution.py:19
  117.9 1.8 copy.262
  121.0 1.3 pad_maximum_fusion.8
  122.3 2.1 %collective-permute-start.6 = (bf16[2,256,256]{2,0,1:T(2,128)(2,1)}, bf16[2,256,256]{2,0,1:T(2,128)(2,1)}, u32[]{:S(2)}, u32[]{:S(2)}) collective-permute-start(bf16[2,256,256]{2,0,1:T(2,128)(2,1)} %pad_maximum_fusion.8), channel_id=1, source_target_pairs={{4,0},{8,4},{12,8},{16,12},{20,16},{24,20},{28,24},{32,28},{36,32}... | collective-permute-start | bytes 786440 | tf_op jit(solution)/shard_map/ppermute | solution.py:19
  124.4 1.8 copy.285
  127.1 1.8 copy.284
  128.9 2.3 %pad_maximum_fusion.9 = bf16[2,256,256]{2,0,1:T(2,128)(2,1)} fusion(bf16[1,256,256]{2,0,1:T(2,128)(2,1)} %copy.285, bf16[1,256,256]{2,0,1:T(2,128)(2,1)} %copy.284), kind=kLoop, calls=%fused_computation.118 | loop fusion | flops 524288 | bytes 524288 | tf_op jit(solution)/shard_map/stack | solution.py:108
  131.3 25.7 %collective-permute-start.7 = (bf16[2,256,256]{2,0,1:T(2,128)(2,1)}, bf16[2,256,256]{2,0,1:T(2,128)(2,1)}, u32[]{:S(2)}, u32[]{:S(2)}) collective-permute-start(bf16[2,256,256]{2,0,1:T(2,128)(2,1)} %pad_maximum_fusion.9), channel_id=1, source_target_pairs={{8,0},{12,4},{16,8},{20,12},{24,16},{28,20},{32,24},{36,28},{40,32... | collective-permute-start | bytes 786440 | tf_op jit(solution)/shard_map/ppermute | solution.py:19
  158.6 1.7 reduce.1
  161.3 3.6 %all-to-all-start.2 = ((bf16[4,2,16384]{2,1,0:T(2,128)(2,1)}), bf16[4,2,16384]{2,1,0:T(2,128)(2,1)S(1)}, u32[]{:S(2)}, u32[]{:S(2)}) async-start(bf16[4,2,16384]{2,1,0:T(2,128)(2,1)} %reshape.273), calls=%async_computation.2 | async-start | bytes 524288 | tf_op jit(solution)/shard_map/all_to_all | solution.py:120
  168.1 12.0 %all-to-all-done.2 = bf16[4,2,16384]{2,1,0:T(2,128)(2,1)S(1)} async-done(((bf16[4,2,16384]{2,1,0:T(2,128)(2,1)}), bf16[4,2,16384]{2,1,0:T(2,128)(2,1)S(1)}, u32[]{:S(2)}, u32[]{:S(2)}) %all-to-all-start.2) | async-done | bytes 262176 | tf_op jit(solution)/shard_map/all_to_all | solution.py:120
  180.1 3.4 %all-to-all-start.5 = ((bf16[4,2,16384]{2,1,0:T(2,128)(2,1)}), bf16[4,2,16384]{2,1,0:T(2,128)(2,1)S(1)}, u32[]{:S(2)}, u32[]{:S(2)}) async-start(bf16[4,2,16384]{2,1,0:T(2,128)(2,1)} %reshape.271), calls=%async_computation.5 | async-start | bytes 524288 | tf_op jit(solution)/shard_map/all_to_all | solution.py:120
  184.9 2.4 %fusion.67 = bf16[256,1,2,256]{3,2,1,0:T(2,128)(2,1)} fusion(bf16[2,256,256]{2,0,1:T(2,128)(2,1)} %collective-permute-done.5, bf16[2,256,256]{2,0,1:T(2,128)(2,1)} %collective-permute-done.4, f32[1,256,256]{2,0,1:T(1,128)S(1)} %copy-done.26, f32[1,256,256]{2,0,1:T(1,128)S(1)} %copy-done.27), kind=kLoop, calls=%fused_computation.128 | loop fusion | flops 786432 | bytes 1310720 | tf_op jit(solution)/shard_map/broadcast_in_dim | solution.py:123
  187.3 2.2 %all-to-all-done.5 = bf16[4,2,16384]{2,1,0:T(2,128)(2,1)S(1)} async-done(((bf16[4,2,16384]{2,1,0:T(2,128)(2,1)}), bf16[4,2,16384]{2,1,0:T(2,128)(2,1)S(1)}, u32[]{:S(2)}, u32[]{:S(2)}) %all-to-all-start.5) | async-done | bytes 262176 | tf_op jit(solution)/shard_map/all_to_all | solution.py:120
  189.5 3.4 %all-to-all-start.6 = ((bf16[256,1,2,256]{3,2,1,0:T(2,128)(2,1)}), bf16[256,1,2,256]{3,2,1,0:T(2,128)(2,1)S(1)}, u32[]{:S(2)}, u32[]{:S(2)}) async-start(bf16[256,1,2,256]{3,2,1,0:T(2,128)(2,1)} %fusion.67), calls=%async_computation.6 | async-start | bytes 524288 | tf_op jit(solution)/shard_map/all_to_all | solution.py:124
  193.4 2.4 %fusion.66 = bf16[256,1,2,256]{3,2,1,0:T(2,128)(2,1)} fusion(bf16[2,256,256]{2,0,1:T(2,128)(2,1)} %collective-permute-done.7, bf16[2,256,256]{2,0,1:T(2,128)(2,1)} %collective-permute-done.6, f32[1,256,256]{2,0,1:T(1,128)S(1)} %copy.277, f32[1,256,256]{2,0,1:T(1,128)S(1)} %copy.276), kind=kLoop, calls=%fused_computation.127 | loop fusion | flops 786432 | bytes 1310720 | tf_op jit(solution)/shard_map/broadcast_in_dim | solution.py:123
  195.8 3.1 %all-to-all-done.6 = bf16[256,1,2,256]{3,2,1,0:T(2,128)(2,1)S(1)} async-done(((bf16[256,1,2,256]{3,2,1,0:T(2,128)(2,1)}), bf16[256,1,2,256]{3,2,1,0:T(2,128)(2,1)S(1)}, u32[]{:S(2)}, u32[]{:S(2)}) %all-to-all-start.6) | async-done | bytes 262176 | tf_op jit(solution)/shard_map/all_to_all | solution.py:124
  198.9 3.4 %all-to-all-start.7 = ((bf16[256,1,2,256]{3,2,1,0:T(2,128)(2,1)}), bf16[256,1,2,256]{3,2,1,0:T(2,128)(2,1)S(1)}, u32[]{:S(2)}, u32[]{:S(2)}) async-start(bf16[256,1,2,256]{3,2,1,0:T(2,128)(2,1)} %fusion.66), calls=%async_computation.7 | async-start | bytes 524288 | tf_op jit(solution)/shard_map/all_to_all | solution.py:124
  203.6 1.2 reshape.240
  204.8 3.4 %all-to-all-done.7 = bf16[256,1,2,256]{3,2,1,0:T(2,128)(2,1)S(1)} async-done(((bf16[256,1,2,256]{3,2,1,0:T(2,128)(2,1)}), bf16[256,1,2,256]{3,2,1,0:T(2,128)(2,1)S(1)}, u32[]{:S(2)}, u32[]{:S(2)}) %all-to-all-start.7) | async-done | bytes 262176 | tf_op jit(solution)/shard_map/all_to_all | solution.py:124
  (216 shorter events, 52.2 us)
Async XLA Ops:
  0.6 1.2 copy-start.43
  3.4 4.5 %copy-start.39 = (bf16[64,4096]{1,0:T(8,128)(2,1)S(1)}, bf16[64,4096]{1,0:T(8,128)(2,1)}, u32[]{:S(2)}) copy-start(bf16[64,4096]{1,0:T(8,128)(2,1)} %param.5) | copy-start | bytes 1572868
  4.3 12.8 %all-to-all-start = ((bf16[64,4,2,256]{3,2,0,1:T(2,128)(2,1)}), bf16[64,4,2,256]{3,2,0,1:T(2,128)(2,1)S(1)}, u32[]{:S(2)}, u32[]{:S(2)}) async-start(bf16[64,4,2,256]{3,2,0,1:T(2,128)(2,1)} %copy.203), calls=%async_computation | async-start | bytes 524288 | tf_op jit(solution)/shard_map/all_to_all | solution.py:29
  17.1 12.2 %all-to-all-start.3 = ((bf16[64,4,2,256]{3,2,0,1:T(2,128)(2,1)}), bf16[64,4,2,256]{3,2,0,1:T(2,128)(2,1)S(1)}, u32[]{:S(2)}, u32[]{:S(2)}) async-start(bf16[64,4,2,256]{3,2,0,1:T(2,128)(2,1)} %copy.231), calls=%async_computation.3 | async-start | bytes 524288 | tf_op jit(solution)/shard_map/all_to_all | solution.py:29
  22.1 46.0 %copy-start.33 = (pred[256,256]{0,1:T(8,128)(4,1)}, pred[256,256]{0,1:T(8,128)(4,1)S(1)}, u32[]{:S(2)}) copy-start(pred[256,256]{0,1:T(8,128)(4,1)S(1)} %get-tuple-element.57) | copy-start | bytes 196612
  22.1 20.8 %collective-permute-start = (bf16[2,256,256]{2,1,0:T(8,128)(2,1)S(1)}, bf16[2,256,256]{2,1,0:T(8,128)(2,1)S(1)}, u32[]{:S(2)}, u32[]{:S(2)}) collective-permute-start(bf16[2,256,256]{2,1,0:T(8,128)(2,1)S(1)} %bitcast.375), channel_id=1, source_target_pairs={{0,8},{4,12},{8,16},{12,20},{16,24},{20,28},{24,32},{28,36},{32,40... | collective-permute-start | bytes 786440 | tf_op jit(solution)/shard_map/ppermute | solution.py:19
  25.8 18.8 %collective-permute-start.1 = (bf16[2,256,256]{2,1,0:T(8,128)(2,1)S(1)}, bf16[2,256,256]{2,1,0:T(8,128)(2,1)S(1)}, u32[]{:S(2)}, u32[]{:S(2)}) collective-permute-start(bf16[2,256,256]{2,1,0:T(8,128)(2,1)S(1)} %bitcast.377), channel_id=1, source_target_pairs={{0,4},{4,8},{8,12},{12,16},{16,20},{20,24},{24,28},{28,32},{32,36}... | collective-permute-start | bytes 786440 | tf_op jit(solution)/shard_map/ppermute | solution.py:19
  29.3 34.8 %all-to-all-start.1 = ((bf16[64,4,2,512]{3,2,0,1:T(2,128)(2,1)}), bf16[64,4,2,512]{3,2,0,1:T(2,128)(2,1)S(1)}, u32[]{:S(2)}, u32[]{:S(2)}) async-start(bf16[64,4,2,512]{3,2,0,1:T(2,128)(2,1)} %copy.206), calls=%async_computation.1 | async-start | bytes 1048576 | tf_op jit(solution)/shard_map/all_to_all | solution.py:41
  32.8 17.5 %collective-permute-start.3 = (bf16[2,256,256]{2,1,0:T(8,128)(2,1)S(1)}, bf16[2,256,256]{2,1,0:T(8,128)(2,1)S(1)}, u32[]{:S(2)}, u32[]{:S(2)}) collective-permute-start(bf16[2,256,256]{2,1,0:T(8,128)(2,1)S(1)} %bitcast.373), channel_id=1, source_target_pairs={{0,4},{4,8},{8,12},{12,16},{16,20},{20,24},{24,28},{28,32},{32,36}... | collective-permute-start | bytes 786440 | tf_op jit(solution)/shard_map/ppermute | solution.py:19
  36.3 25.4 %collective-permute-start.2 = (bf16[2,256,256]{2,1,0:T(8,128)(2,1)S(1)}, bf16[2,256,256]{2,1,0:T(8,128)(2,1)S(1)}, u32[]{:S(2)}, u32[]{:S(2)}) collective-permute-start(bf16[2,256,256]{2,1,0:T(8,128)(2,1)S(1)} %bitcast.374), channel_id=1, source_target_pairs={{0,8},{4,12},{8,16},{12,20},{16,24},{20,28},{24,32},{28,36},{32,40... | collective-permute-start | bytes 786440 | tf_op jit(solution)/shard_map/ppermute | solution.py:19
  41.3 26.9 %copy-start.16 = (bf16[1,256,256]{1,2,0:T(8,128)(2,1)}, bf16[1,256,256]{1,2,0:T(8,128)(2,1)S(1)}, u32[]{:S(2)}) copy-start(bf16[1,256,256]{1,2,0:T(8,128)(2,1)S(1)} %copy.211) | copy-start | bytes 393220
  45.4 24.0 %copy-start.20 = (bf16[1,256,256]{1,2,0:T(8,128)(2,1)}, bf16[1,256,256]{1,2,0:T(8,128)(2,1)S(1)}, u32[]{:S(2)}) copy-start(bf16[1,256,256]{1,2,0:T(8,128)(2,1)S(1)} %copy.214) | copy-start | bytes 393220
  64.0 16.1 %all-to-all-start.4 = ((bf16[64,4,2,512]{3,2,0,1:T(2,128)(2,1)}), bf16[64,4,2,512]{3,2,0,1:T(2,128)(2,1)S(1)}, u32[]{:S(2)}, u32[]{:S(2)}) async-start(bf16[64,4,2,512]{3,2,0,1:T(2,128)(2,1)} %copy.234), calls=%async_computation.4 | async-start | bytes 1048576 | tf_op jit(solution)/shard_map/all_to_all | solution.py:41
  68.0 1.5 copy-start.6
  70.2 6.9 %copy-start = (f32[2,2,256,256]{2,3,1,0:T(8,128)}, f32[2,2,256,256]{2,3,1,0:T(8,128)S(1)}, u32[]{:S(2)}) copy-start(f32[2,2,256,256]{2,3,1,0:T(8,128)S(1)} %get-tuple-element.72) | copy-start | bytes 3145732
  70.3 6.3 %copy-start.44 = (f32[2,2,256]{2,1,0:T(2,128)}, f32[2,2,256]{2,1,0:T(2,128)S(1)}, u32[]{:S(2)}) copy-start(f32[2,2,256]{2,1,0:T(2,128)S(1)} %get-tuple-element.17) | copy-start | bytes 12292
  70.3 6.3 %copy-start.46 = (f32[2,2,256]{2,1,0:T(2,128)}, f32[2,2,256]{2,1,0:T(2,128)S(1)}, u32[]{:S(2)}) copy-start(f32[2,2,256]{2,1,0:T(2,128)S(1)} %get-tuple-element.18) | copy-start | bytes 12292
  70.8 2.0 copy-start.38
  72.7 1.9 copy-start.37
  81.1 1.3 copy-start.18
  81.1 1.3 copy-start.32
  82.4 1.4 copy-start.24
  82.4 1.4 copy-start.30
  88.2 1.5 copy-start.2
  88.2 1.5 copy-start.4
  88.2 1.5 copy-start.35
  89.7 1.2 copy-start.3
  89.8 1.2 copy-start.34
  91.0 3.1 %copy-start.11 = (f32[2,2,256,256]{2,3,1,0:T(8,128)S(1)}, f32[2,2,256,256]{2,3,1,0:T(8,128)}, u32[]{:S(2)}) copy-start(f32[2,2,256,256]{2,3,1,0:T(8,128)} %get-tuple-element.74) | copy-start | bytes 3145732
  91.0 3.1 %copy-start.12 = (f32[2,2,256,256]{2,3,1,0:T(8,128)S(1)}, f32[2,2,256,256]{2,3,1,0:T(8,128)}, u32[]{:S(2)}) copy-start(f32[2,2,256,256]{2,3,1,0:T(8,128)} %get-tuple-element.73) | copy-start | bytes 3145732
  91.4 2.7 %copy-start.10 = (f32[2,2,256,256]{2,3,1,0:T(8,128)S(1)}, f32[2,2,256,256]{2,3,1,0:T(8,128)}, u32[]{:S(2)}) copy-start(f32[2,2,256,256]{2,3,1,0:T(8,128)} %get-tuple-element.75) | copy-start | bytes 3145732
  92.4 1.7 copy-start.1
  94.1 1.4 copy-start.7
  103.5 4.5 %copy-start.9 = (bf16[2,2,256,256]{2,3,1,0:T(8,128)(2,1)S(1)}, bf16[2,2,256,256]{2,3,1,0:T(8,128)(2,1)}, u32[]{:S(2)}) copy-start(bf16[2,2,256,256]{2,3,1,0:T(8,128)(2,1)} %get-tuple-element.49) | copy-start | bytes 1572868
  104.8 3.2 %copy-start.8 = (bf16[256,1,1,512]{0,3,2,1:T(8,128)(2,1)S(1)}, bf16[256,1,1,512]{0,3,2,1:T(8,128)(2,1)}, u32[]{:S(2)}) copy-start(bf16[256,1,1,512]{0,3,2,1:T(8,128)(2,1)} %copy-done.6) | copy-start | bytes 786436
  104.8 79.2 %collective-permute-start.4 = (bf16[2,256,256]{2,0,1:T(2,128)(2,1)}, bf16[2,256,256]{2,0,1:T(2,128)(2,1)}, u32[]{:S(2)}, u32[]{:S(2)}) collective-permute-start(bf16[2,256,256]{2,0,1:T(2,128)(2,1)} %pad_maximum_fusion.6), channel_id=1, source_target_pairs={{4,0},{8,4},{12,8},{16,12},{20,16},{24,20},{28,24},{32,28},{36,32}... | collective-permute-start | bytes 786440 | tf_op jit(solution)/shard_map/ppermute | solution.py:19
  111.3 72.7 %collective-permute-start.5 = (bf16[2,256,256]{2,0,1:T(2,128)(2,1)}, bf16[2,256,256]{2,0,1:T(2,128)(2,1)}, u32[]{:S(2)}, u32[]{:S(2)}) collective-permute-start(bf16[2,256,256]{2,0,1:T(2,128)(2,1)} %pad_maximum_fusion.7), channel_id=1, source_target_pairs={{8,0},{12,4},{16,8},{20,12},{24,16},{28,20},{32,24},{36,28},{40,32... | collective-permute-start | bytes 786440 | tf_op jit(solution)/shard_map/ppermute | solution.py:19
  117.9 1.8 copy-start.42
  122.3 71.2 %collective-permute-start.6 = (bf16[2,256,256]{2,0,1:T(2,128)(2,1)}, bf16[2,256,256]{2,0,1:T(2,128)(2,1)}, u32[]{:S(2)}, u32[]{:S(2)}) collective-permute-start(bf16[2,256,256]{2,0,1:T(2,128)(2,1)} %pad_maximum_fusion.8), channel_id=1, source_target_pairs={{4,0},{8,4},{12,8},{16,12},{20,16},{24,20},{28,24},{32,28},{36,32}... | collective-permute-start | bytes 786440 | tf_op jit(solution)/shard_map/ppermute | solution.py:19
  127.1 29.9 %copy-start.14 = (f32[2,128,2,256]{3,1,2,0:T(8,128)S(1)}, f32[2,128,2,256]{3,1,2,0:T(8,128)}, u32[]{:S(2)}) copy-start(f32[2,128,2,256]{3,1,2,0:T(8,128)} %fusion.89) | copy-start | bytes 1572868
  128.9 28.1 %copy-start.13 = (f32[2,128,2,256]{3,1,2,0:T(8,128)S(1)}, f32[2,128,2,256]{3,1,2,0:T(8,128)}, u32[]{:S(2)}) copy-start(f32[2,128,2,256]{3,1,2,0:T(8,128)} %fusion.88) | copy-start | bytes 1572868
  128.9 28.1 %copy-start.23 = (bf16[1,256,256]{1,2,0:T(8,128)(2,1)S(1)}, bf16[1,256,256]{1,2,0:T(8,128)(2,1)}, u32[]{:S(2)}) copy-start(bf16[1,256,256]{1,2,0:T(8,128)(2,1)} %copy.205) | copy-start | bytes 393220
  131.3 62.1 %collective-permute-start.7 = (bf16[2,256,256]{2,0,1:T(2,128)(2,1)}, bf16[2,256,256]{2,0,1:T(2,128)(2,1)}, u32[]{:S(2)}, u32[]{:S(2)}) collective-permute-start(bf16[2,256,256]{2,0,1:T(2,128)(2,1)} %pad_maximum_fusion.9), channel_id=1, source_target_pairs={{8,0},{12,4},{16,8},{20,12},{24,16},{28,20},{32,24},{36,28},{40,32... | collective-permute-start | bytes 786440 | tf_op jit(solution)/shard_map/ppermute | solution.py:19
  161.3 18.8 %all-to-all-start.2 = ((bf16[4,2,16384]{2,1,0:T(2,128)(2,1)}), bf16[4,2,16384]{2,1,0:T(2,128)(2,1)S(1)}, u32[]{:S(2)}, u32[]{:S(2)}) async-start(bf16[4,2,16384]{2,1,0:T(2,128)(2,1)} %reshape.273), calls=%async_computation.2 | async-start | bytes 524288 | tf_op jit(solution)/shard_map/all_to_all | solution.py:120
  168.1 15.4 %copy-start.5 = (bf16[256,1,1,512]{0,3,2,1:T(8,128)(2,1)S(1)}, bf16[256,1,1,512]{0,3,2,1:T(8,128)(2,1)}, u32[]{:S(2)}) copy-start(bf16[256,1,1,512]{0,3,2,1:T(8,128)(2,1)} %copy.246) | copy-start | bytes 786436
  180.1 9.4 %all-to-all-start.5 = ((bf16[4,2,16384]{2,1,0:T(2,128)(2,1)}), bf16[4,2,16384]{2,1,0:T(2,128)(2,1)S(1)}, u32[]{:S(2)}, u32[]{:S(2)}) async-start(bf16[4,2,16384]{2,1,0:T(2,128)(2,1)} %reshape.271), calls=%async_computation.5 | async-start | bytes 524288 | tf_op jit(solution)/shard_map/all_to_all | solution.py:120
  189.5 9.4 %all-to-all-start.6 = ((bf16[256,1,2,256]{3,2,1,0:T(2,128)(2,1)}), bf16[256,1,2,256]{3,2,1,0:T(2,128)(2,1)S(1)}, u32[]{:S(2)}, u32[]{:S(2)}) async-start(bf16[256,1,2,256]{3,2,1,0:T(2,128)(2,1)} %fusion.67), calls=%async_computation.6 | async-start | bytes 524288 | tf_op jit(solution)/shard_map/all_to_all | solution.py:124
  198.9 9.4 %all-to-all-start.7 = ((bf16[256,1,2,256]{3,2,1,0:T(2,128)(2,1)}), bf16[256,1,2,256]{3,2,1,0:T(2,128)(2,1)S(1)}, u32[]{:S(2)}, u32[]{:S(2)}) async-start(bf16[256,1,2,256]{3,2,1,0:T(2,128)(2,1)} %fusion.66), calls=%async_computation.7 | async-start | bytes 524288 | tf_op jit(solution)/shard_map/all_to_all | solution.py:124
  (22 other events, 20.6 us)
where the time goes:
time: 212 us; the launch traced here: 211 us
  starting transfers between devices  79.9 us (38%)
  local copies, waits for them, and re-layouts  43.9 us (21%)
  waiting for transfers between devices  36.4 us (17%)
  matrix products  27.9 us (13%)
  other arithmetic  21 us (10%)
    ppermute x8, starting transfers between devices, passed_along(): return lax.ppermute(block, axis, route)  51.8 us
    ppermute x8, waiting for transfers between devices, passed_along(): return lax.ppermute(block, axis, route)  15.7 us
    all_to_all x2, waiting for transfers between devices, attend_chunk(): lax.all_to_all(grad_query_loc.astype(jnp.bfloat16), 'head', split_axis=0,...  14.2 us
    another operation x12, local copies, waits for them, and re-layouts, attend_chunk(): jnp.stack([key_part, value_part]).reshape(2, tok_rows, kv_cols)  10.3 us
    unnamed x116, local copies, waits for them, and re-layouts  10.1 us
    all_to_all x2, starting transfers between devices, attend_chunk(): lax.all_to_all(qg_in, 'head', split_axis=1, concat_axis=0, tiled=True)  7.13 us
    all_to_all x2, starting transfers between devices, attend_chunk(): lax.all_to_all(kv_in, 'head', split_axis=1, concat_axis=0, tiled=True)  7.07 us
    all_to_all x2, starting transfers between devices, attend_chunk(): lax.all_to_all(grad_query_loc.astype(jnp.bfloat16), 'head', split_axis=0,...  7.05 us
  transfers between devices with their start and end apart: 16, of which 7 were waited for; matrix products, arithmetic and copies ran while one was open for 27% of the time, Pallas kernels for 0%

commit v1 on v0

--- a/solution.py
+++ b/solution.py
@@ -117,8 +117,16 @@
                 kv_parts[distance].astype(jnp.bfloat16), "ctx", -distance
             )
     grad_query_loc = query_total.reshape(tok_rows, 1, kv_groups * group_share * HEAD_SIZE)
-    grad_q = lax.all_to_all(
-        grad_query_loc.astype(jnp.bfloat16), "head", split_axis=0, concat_axis=1, tiled=True
+    grad_q = jnp.concatenate(
+        lax.all_to_all(
+            jnp.stack(
+                jnp.split(grad_query_loc.astype(jnp.bfloat16), lax.axis_size("head"), axis=0)
+            ),
+            "head",
+            0,
+            0,
+        ),
+        axis=1,
     )
     kv_out = jnp.moveaxis(kv_total.astype(jnp.bfloat16), 0, 1)[:, None]
     kv_back = lax.all_to_all(kv_out, "head", split_axis=0, concat_axis=1, tiled=True)

time: 212 us -> 216 us (1.019)
  local copies, waits for them, and re-layouts: 43.9 us -> 47 us
    another operation x12, local copies, waits for them, and re-layouts: 10.3 us -> 16.2 us  [attend_chunk(): jnp.stack([key_part, value_part]).reshape(2, tok_rows, kv_cols)]
    unnamed x116 -> x104, local copies, waits for them, and re-layouts: 10.1 us -> 6.85 us
    another operation x4, other arithmetic: 6.26 us -> 9.2 us  [attend_chunk(): jnp.stack([key_part, value_part]).reshape(2, tok_rows, kv_cols)]
    convert_element_type x2 -> x0, other arithmetic: 2.55 us -> none  [attend_chunk(): grad_query_loc.astype(jnp.bfloat16)]
  transfers between devices with their start and end apart: 16 -> 16, of which waited for: 7 -> 7; matrix products, arithmetic and copies ran while one was open for 27% -> 28% of each run, Pallas kernels for 0% -> 0%
where the time goes in v1:
time: 216 us; the launch traced here: 215 us
  starting transfers between devices  79.8 us (37%)
  local copies, waits for them, and re-layouts  47 us (22%)
  waiting for transfers between devices  36.6 us (17%)
  matrix products  27 us (12%)
  other arithmetic  22.8 us (11%)
    ppermute x8, starting transfers between devices, passed_along(): return lax.ppermute(block, axis, route)  51.7 us
    another operation x12, local copies, waits for them, and re-layouts, attend_chunk(): jnp.stack([key_part, value_part]).reshape(2, tok_rows, kv_cols)  16.2 us
    ppermute x8, waiting for transfers between devices, passed_along(): return lax.ppermute(block, axis, route)  15.7 us
    all_to_all x2, waiting for transfers between devices, attend_chunk(): lax.all_to_all(jnp.stack(jnp.split(grad_query_loc.astype(jnp.bfloat16), l...  13.7 us
    another operation x4, other arithmetic, attend_chunk(): jnp.stack([key_part, value_part]).reshape(2, tok_rows, kv_cols)  9.2 us
    all_to_all x2, waiting for transfers between devices, attend_chunk(): lax.all_to_all(kv_out, 'head', split_axis=0, concat_axis=1, tiled=True)  7.18 us
    all_to_all x2, starting transfers between devices, attend_chunk(): lax.all_to_all(qg_in, 'head', split_axis=1, concat_axis=0, tiled=True)  7.13 us
    all_to_all x2, starting transfers between devices, attend_chunk(): lax.all_to_all(kv_in, 'head', split_axis=1, concat_axis=0, tiled=True)  7.07 us
  transfers between devices with their start and end apart: 16, of which 7 were waited for; matrix products, arithmetic and copies ran while one was open for 28% of the time, Pallas kernels for 0%

profile of v1, /device:TPU:184, one launch (start us, length us, event | category | flops | bytes accessed | tf_op | source)
XLA Modules:
  0.0 214.7 jit_solution(13384049019158558989)
XLA Ops:
  4.3 3.6 %all-to-all-start = ((bf16[64,4,2,256]{3,2,0,1:T(2,128)(2,1)}), bf16[64,4,2,256]{3,2,0,1:T(2,128)(2,1)S(1)}, u32[]{:S(2)}, u32[]{:S(2)}) async-start(bf16[64,4,2,256]{3,2,0,1:T(2,128)(2,1)} %copy.291), calls=%async_computation | async-start | bytes 524288 | tf_op jit(solution)/shard_map/all_to_all | solution.py:29
  9.3 1.5 fusion.73
  10.8 1.2 pad_maximum_fusion
  17.1 3.4 %all-to-all-start.3 = ((bf16[64,4,2,256]{3,2,0,1:T(2,128)(2,1)}), bf16[64,4,2,256]{3,2,0,1:T(2,128)(2,1)S(1)}, u32[]{:S(2)}, u32[]{:S(2)}) async-start(bf16[64,4,2,256]{3,2,0,1:T(2,128)(2,1)} %copy.322), calls=%async_computation.3 | async-start | bytes 524288 | tf_op jit(solution)/shard_map/all_to_all | solution.py:29
  22.1 3.6 %collective-permute-start = (bf16[2,256,256]{2,1,0:T(8,128)(2,1)S(1)}, bf16[2,256,256]{2,1,0:T(8,128)(2,1)S(1)}, u32[]{:S(2)}, u32[]{:S(2)}) collective-permute-start(bf16[2,256,256]{2,1,0:T(8,128)(2,1)S(1)} %bitcast.375), channel_id=1, source_target_pairs={{0,8},{4,12},{8,16},{12,20},{16,24},{20,28},{24,32},{28,36},{32,40... | collective-permute-start | bytes 786440 | tf_op jit(solution)/shard_map/ppermute | solution.py:19
  25.8 3.5 %collective-permute-start.1 = (bf16[2,256,256]{2,1,0:T(8,128)(2,1)S(1)}, bf16[2,256,256]{2,1,0:T(8,128)(2,1)S(1)}, u32[]{:S(2)}, u32[]{:S(2)}) collective-permute-start(bf16[2,256,256]{2,1,0:T(8,128)(2,1)S(1)} %bitcast.377), channel_id=1, source_target_pairs={{0,4},{4,8},{8,12},{12,16},{16,20},{20,24},{24,28},{28,32},{32,36}... | collective-permute-start | bytes 786440 | tf_op jit(solution)/shard_map/ppermute | solution.py:19
  29.3 3.5 %all-to-all-start.1 = ((bf16[64,4,2,512]{3,2,0,1:T(2,128)(2,1)}), bf16[64,4,2,512]{3,2,0,1:T(2,128)(2,1)S(1)}, u32[]{:S(2)}, u32[]{:S(2)}) async-start(bf16[64,4,2,512]{3,2,0,1:T(2,128)(2,1)} %copy.294), calls=%async_computation.1 | async-start | bytes 1048576 | tf_op jit(solution)/shard_map/all_to_all | solution.py:41
  32.8 3.5 %collective-permute-start.3 = (bf16[2,256,256]{2,1,0:T(8,128)(2,1)S(1)}, bf16[2,256,256]{2,1,0:T(8,128)(2,1)S(1)}, u32[]{:S(2)}, u32[]{:S(2)}) collective-permute-start(bf16[2,256,256]{2,1,0:T(8,128)(2,1)S(1)} %bitcast.373), channel_id=1, source_target_pairs={{0,4},{4,8},{8,12},{12,16},{16,20},{20,24},{24,28},{28,32},{32,36}... | collective-permute-start | bytes 786440 | tf_op jit(solution)/shard_map/ppermute | solution.py:19
  36.3 4.8 %collective-permute-start.2 = (bf16[2,256,256]{2,1,0:T(8,128)(2,1)S(1)}, bf16[2,256,256]{2,1,0:T(8,128)(2,1)S(1)}, u32[]{:S(2)}, u32[]{:S(2)}) collective-permute-start(bf16[2,256,256]{2,1,0:T(8,128)(2,1)S(1)} %bitcast.374), channel_id=1, source_target_pairs={{0,8},{4,12},{8,16},{12,20},{16,24},{20,28},{24,32},{28,36},{32,40... | collective-permute-start | bytes 786440 | tf_op jit(solution)/shard_map/ppermute | solution.py:19
  42.9 1.7 collective-permute-done.1
  47.0 3.4 %collective-permute-done.3 = bf16[2,256,256]{2,1,0:T(8,128)(2,1)S(1)} collective-permute-done((bf16[2,256,256]{2,1,0:T(8,128)(2,1)S(1)}, bf16[2,256,256]{2,1,0:T(8,128)(2,1)S(1)}, u32[]{:S(2)}, u32[]{:S(2)}) %collective-permute-start.3) | collective-permute-done | bytes 262176 | tf_op jit(solution)/shard_map/ppermute | solution.py:19
  51.1 10.6 %collective-permute-done.2 = bf16[2,256,256]{2,1,0:T(8,128)(2,1)S(1)} collective-permute-done((bf16[2,256,256]{2,1,0:T(8,128)(2,1)S(1)}, bf16[2,256,256]{2,1,0:T(8,128)(2,1)S(1)}, u32[]{:S(2)}, u32[]{:S(2)}) %collective-permute-start.2) | collective-permute-done | bytes 262176 | tf_op jit(solution)/shard_map/ppermute | solution.py:19
  64.0 3.7 %all-to-all-start.4 = ((bf16[64,4,2,512]{3,2,0,1:T(2,128)(2,1)}), bf16[64,4,2,512]{3,2,0,1:T(2,128)(2,1)S(1)}, u32[]{:S(2)}, u32[]{:S(2)}) async-start(bf16[64,4,2,512]{3,2,0,1:T(2,128)(2,1)} %copy.325), calls=%async_computation.4 | async-start | bytes 1048576 | tf_op jit(solution)/shard_map/all_to_all | solution.py:41
  70.7 1.9 multiply_reduce_fusion.5
  72.7 1.9 multiply_reduce_fusion.4
  74.6 1.9 multiply_reduce_fusion.3
  81.0 1.2 fusion.87
  82.3 1.3 fusion.88
  83.7 1.9 fusion.86
  85.6 1.8 copy.337
  88.1 1.5 multiply_reduce_fusion.2
  94.0 1.4 multiply_convert_fusion.5
  103.1 1.8 copy.360
  105.0 2.3 %pad_maximum_fusion.8 = bf16[2,256,256]{2,0,1:T(2,128)(2,1)} fusion(bf16[1,256,256]{2,0,1:T(2,128)(2,1)} %copy.361, bf16[1,256,256]{2,0,1:T(2,128)(2,1)} %copy.360), kind=kLoop, calls=%fused_computation.119 | loop fusion | flops 524288 | bytes 524288 | tf_op jit(solution)/shard_map/stack | solution.py:108
  107.3 1.9 collective-permute-start.4
  110.2 1.8 copy.364
  111.9 1.8 copy.365
  113.7 2.3 %pad_maximum_fusion.9 = bf16[2,256,256]{2,0,1:T(2,128)(2,1)} fusion(bf16[1,256,256]{2,0,1:T(2,128)(2,1)} %copy.365, bf16[1,256,256]{2,0,1:T(2,128)(2,1)} %copy.364), kind=kLoop, calls=%fused_computation.120 | loop fusion | flops 524288 | bytes 524288 | tf_op jit(solution)/shard_map/stack | solution.py:108
  116.0 6.5 %collective-permute-start.5 = (bf16[2,256,256]{2,0,1:T(2,128)(2,1)}, bf16[2,256,256]{2,0,1:T(2,128)(2,1)}, u32[]{:S(2)}, u32[]{:S(2)}) collective-permute-start(bf16[2,256,256]{2,0,1:T(2,128)(2,1)} %pad_maximum_fusion.9), channel_id=1, source_target_pairs={{8,0},{12,4},{16,8},{20,12},{24,16},{28,20},{32,24},{36,28},{40,32... | collective-permute-start | bytes 786440 | tf_op jit(solution)/shard_map/ppermute | solution.py:19
  122.5 1.8 copy.356
  124.3 1.8 copy.375
  126.1 1.8 copy.374
  127.8 2.3 %pad_maximum_fusion.10 = bf16[2,256,256]{2,0,1:T(2,128)(2,1)} fusion(bf16[1,256,256]{2,0,1:T(2,128)(2,1)} %copy.375, bf16[1,256,256]{2,0,1:T(2,128)(2,1)} %copy.374), kind=kLoop, calls=%fused_computation.121 | loop fusion | flops 524288 | bytes 524288 | tf_op jit(solution)/shard_map/stack | solution.py:108
  130.1 1.9 collective-permute-start.6
  132.0 1.8 copy.379
  134.8 1.8 copy.378
  136.5 2.3 %pad_maximum_fusion.11 = bf16[2,256,256]{2,0,1:T(2,128)(2,1)} fusion(bf16[1,256,256]{2,0,1:T(2,128)(2,1)} %copy.379, bf16[1,256,256]{2,0,1:T(2,128)(2,1)} %copy.378), kind=kLoop, calls=%fused_computation.122 | loop fusion | flops 524288 | bytes 524288 | tf_op jit(solution)/shard_map/stack | solution.py:108
  138.9 26.0 %collective-permute-start.7 = (bf16[2,256,256]{2,0,1:T(2,128)(2,1)}, bf16[2,256,256]{2,0,1:T(2,128)(2,1)}, u32[]{:S(2)}, u32[]{:S(2)}) collective-permute-start(bf16[2,256,256]{2,0,1:T(2,128)(2,1)} %pad_maximum_fusion.11), channel_id=1, source_target_pairs={{8,0},{12,4},{16,8},{20,12},{24,16},{28,20},{32,24},{36,28},{40,32... | collective-permute-start | bytes 786440 | tf_op jit(solution)/shard_map/ppermute | solution.py:19
  166.4 3.7 %all-to-all-start.2 = ((bf16[4,64,1,512]{3,1,2,0:T(8,128)(2,1)}), bf16[4,64,1,512]{3,1,2,0:T(8,128)(2,1)S(1)}, u32[]{:S(2)}, u32[]{:S(2)}) async-start(bf16[4,64,1,512]{3,1,2,0:T(8,128)(2,1)} %pad_maximum_fusion.5), calls=%async_computation.2 | async-start | bytes 524288 | tf_op jit(solution)/shard_map/all_to_all | solution.py:121
  172.6 11.5 %all-to-all-done.2 = bf16[4,64,1,512]{3,1,2,0:T(8,128)(2,1)S(1)} async-done(((bf16[4,64,1,512]{3,1,2,0:T(8,128)(2,1)}), bf16[4,64,1,512]{3,1,2,0:T(8,128)(2,1)S(1)}, u32[]{:S(2)}, u32[]{:S(2)}) %all-to-all-start.2) | async-done | bytes 262176 | tf_op jit(solution)/shard_map/all_to_all | solution.py:121
  184.1 3.4 %all-to-all-start.5 = ((bf16[4,64,1,512]{3,1,2,0:T(8,128)(2,1)}), bf16[4,64,1,512]{3,1,2,0:T(8,128)(2,1)S(1)}, u32[]{:S(2)}, u32[]{:S(2)}) async-start(bf16[4,64,1,512]{3,1,2,0:T(8,128)(2,1)} %pad_maximum_fusion.7), calls=%async_computation.5 | async-start | bytes 524288 | tf_op jit(solution)/shard_map/all_to_all | solution.py:121
  188.9 2.4 %fusion.69 = bf16[256,1,2,256]{3,2,1,0:T(2,128)(2,1)} fusion(bf16[2,256,256]{2,0,1:T(2,128)(2,1)} %collective-permute-done.5, bf16[2,256,256]{2,0,1:T(2,128)(2,1)} %collective-permute-done.4, f32[1,256,256]{2,0,1:T(1,128)S(1)} %copy-done.25, f32[1,256,256]{2,0,1:T(1,128)S(1)} %copy-done.26), kind=kLoop, calls=%fused_computation.132 | loop fusion | flops 786432 | bytes 1310720 | tf_op jit(solution)/shard_map/broadcast_in_dim | solution.py:131
  191.3 2.2 %all-to-all-done.5 = bf16[4,64,1,512]{3,1,2,0:T(8,128)(2,1)S(1)} async-done(((bf16[4,64,1,512]{3,1,2,0:T(8,128)(2,1)}), bf16[4,64,1,512]{3,1,2,0:T(8,128)(2,1)S(1)}, u32[]{:S(2)}, u32[]{:S(2)}) %all-to-all-start.5) | async-done | bytes 262176 | tf_op jit(solution)/shard_map/all_to_all | solution.py:121
  193.5 3.4 %all-to-all-start.6 = ((bf16[256,1,2,256]{3,2,1,0:T(2,128)(2,1)}), bf16[256,1,2,256]{3,2,1,0:T(2,128)(2,1)S(1)}, u32[]{:S(2)}, u32[]{:S(2)}) async-start(bf16[256,1,2,256]{3,2,1,0:T(2,128)(2,1)} %fusion.69), calls=%async_computation.6 | async-start | bytes 524288 | tf_op jit(solution)/shard_map/all_to_all | solution.py:132
  197.4 2.4 %fusion.68 = bf16[256,1,2,256]{3,2,1,0:T(2,128)(2,1)} fusion(bf16[2,256,256]{2,0,1:T(2,128)(2,1)} %collective-permute-done.7, bf16[2,256,256]{2,0,1:T(2,128)(2,1)} %collective-permute-done.6, f32[1,256,256]{2,0,1:T(1,128)S(1)} %copy.371, f32[1,256,256]{2,0,1:T(1,128)S(1)} %copy.370), kind=kLoop, calls=%fused_computation.131 | loop fusion | flops 786432 | bytes 1310720 | tf_op jit(solution)/shard_map/broadcast_in_dim | solution.py:131
  199.9 3.1 %all-to-all-done.6 = bf16[256,1,2,256]{3,2,1,0:T(2,128)(2,1)S(1)} async-done(((bf16[256,1,2,256]{3,2,1,0:T(2,128)(2,1)}), bf16[256,1,2,256]{3,2,1,0:T(2,128)(2,1)S(1)}, u32[]{:S(2)}, u32[]{:S(2)}) %all-to-all-start.6) | async-done | bytes 262176 | tf_op jit(solution)/shard_map/all_to_all | solution.py:132
  202.9 3.4 %all-to-all-start.7 = ((bf16[256,1,2,256]{3,2,1,0:T(2,128)(2,1)}), bf16[256,1,2,256]{3,2,1,0:T(2,128)(2,1)S(1)}, u32[]{:S(2)}, u32[]{:S(2)}) async-start(bf16[256,1,2,256]{3,2,1,0:T(2,128)(2,1)} %fusion.68), calls=%async_computation.7 | async-start | bytes 524288 | tf_op jit(solution)/shard_map/all_to_all | solution.py:132
  208.2 4.1 %all-to-all-done.7 = bf16[256,1,2,256]{3,2,1,0:T(2,128)(2,1)S(1)} async-done(((bf16[256,1,2,256]{3,2,1,0:T(2,128)(2,1)}), bf16[256,1,2,256]{3,2,1,0:T(2,128)(2,1)S(1)}, u32[]{:S(2)}, u32[]{:S(2)}) %all-to-all-start.7) | async-done | bytes 262176 | tf_op jit(solution)/shard_map/all_to_all | solution.py:132
  (213 shorter events, 50.9 us)
Async XLA Ops:
  0.6 1.2 copy-start.41
  3.4 4.5 %copy-start.38 = (bf16[64,4096]{1,0:T(8,128)(2,1)S(1)}, bf16[64,4096]{1,0:T(8,128)(2,1)}, u32[]{:S(2)}) copy-start(bf16[64,4096]{1,0:T(8,128)(2,1)} %param.5) | copy-start | bytes 1572868
  4.3 12.8 %all-to-all-start = ((bf16[64,4,2,256]{3,2,0,1:T(2,128)(2,1)}), bf16[64,4,2,256]{3,2,0,1:T(2,128)(2,1)S(1)}, u32[]{:S(2)}, u32[]{:S(2)}) async-start(bf16[64,4,2,256]{3,2,0,1:T(2,128)(2,1)} %copy.291), calls=%async_computation | async-start | bytes 524288 | tf_op jit(solution)/shard_map/all_to_all | solution.py:29
  7.9 1.0 copy-start.39
  17.1 12.2 %all-to-all-start.3 = ((bf16[64,4,2,256]{3,2,0,1:T(2,128)(2,1)}), bf16[64,4,2,256]{3,2,0,1:T(2,128)(2,1)S(1)}, u32[]{:S(2)}, u32[]{:S(2)}) async-start(bf16[64,4,2,256]{3,2,0,1:T(2,128)(2,1)} %copy.322), calls=%async_computation.3 | async-start | bytes 524288 | tf_op jit(solution)/shard_map/all_to_all | solution.py:29
  22.1 46.0 %copy-start.32 = (pred[256,256]{0,1:T(8,128)(4,1)}, pred[256,256]{0,1:T(8,128)(4,1)S(1)}, u32[]{:S(2)}) copy-start(pred[256,256]{0,1:T(8,128)(4,1)S(1)} %get-tuple-element.65) | copy-start | bytes 196612
  22.1 20.7 %collective-permute-start = (bf16[2,256,256]{2,1,0:T(8,128)(2,1)S(1)}, bf16[2,256,256]{2,1,0:T(8,128)(2,1)S(1)}, u32[]{:S(2)}, u32[]{:S(2)}) collective-permute-start(bf16[2,256,256]{2,1,0:T(8,128)(2,1)S(1)} %bitcast.375), channel_id=1, source_target_pairs={{0,8},{4,12},{8,16},{12,20},{16,24},{20,28},{24,32},{28,36},{32,40... | collective-permute-start | bytes 786440 | tf_op jit(solution)/shard_map/ppermute | solution.py:19
  25.8 18.8 %collective-permute-start.1 = (bf16[2,256,256]{2,1,0:T(8,128)(2,1)S(1)}, bf16[2,256,256]{2,1,0:T(8,128)(2,1)S(1)}, u32[]{:S(2)}, u32[]{:S(2)}) collective-permute-start(bf16[2,256,256]{2,1,0:T(8,128)(2,1)S(1)} %bitcast.377), channel_id=1, source_target_pairs={{0,4},{4,8},{8,12},{12,16},{16,20},{20,24},{24,28},{28,32},{32,36}... | collective-permute-start | bytes 786440 | tf_op jit(solution)/shard_map/ppermute | solution.py:19
  29.3 34.7 %all-to-all-start.1 = ((bf16[64,4,2,512]{3,2,0,1:T(2,128)(2,1)}), bf16[64,4,2,512]{3,2,0,1:T(2,128)(2,1)S(1)}, u32[]{:S(2)}, u32[]{:S(2)}) async-start(bf16[64,4,2,512]{3,2,0,1:T(2,128)(2,1)} %copy.294), calls=%async_computation.1 | async-start | bytes 1048576 | tf_op jit(solution)/shard_map/all_to_all | solution.py:41
  32.8 17.5 %collective-permute-start.3 = (bf16[2,256,256]{2,1,0:T(8,128)(2,1)S(1)}, bf16[2,256,256]{2,1,0:T(8,128)(2,1)S(1)}, u32[]{:S(2)}, u32[]{:S(2)}) collective-permute-start(bf16[2,256,256]{2,1,0:T(8,128)(2,1)S(1)} %bitcast.373), channel_id=1, source_target_pairs={{0,4},{4,8},{8,12},{12,16},{16,20},{20,24},{24,28},{28,32},{32,36}... | collective-permute-start | bytes 786440 | tf_op jit(solution)/shard_map/ppermute | solution.py:19
  36.3 25.4 %collective-permute-start.2 = (bf16[2,256,256]{2,1,0:T(8,128)(2,1)S(1)}, bf16[2,256,256]{2,1,0:T(8,128)(2,1)S(1)}, u32[]{:S(2)}, u32[]{:S(2)}) collective-permute-start(bf16[2,256,256]{2,1,0:T(8,128)(2,1)S(1)} %bitcast.374), channel_id=1, source_target_pairs={{0,8},{4,12},{8,16},{12,20},{16,24},{20,28},{24,32},{28,36},{32,40... | collective-permute-start | bytes 786440 | tf_op jit(solution)/shard_map/ppermute | solution.py:19
  41.2 26.8 %copy-start.15 = (bf16[1,256,256]{1,2,0:T(8,128)(2,1)}, bf16[1,256,256]{1,2,0:T(8,128)(2,1)S(1)}, u32[]{:S(2)}) copy-start(bf16[1,256,256]{1,2,0:T(8,128)(2,1)S(1)} %copy.299) | copy-start | bytes 393220
  45.4 23.9 %copy-start.19 = (bf16[1,256,256]{1,2,0:T(8,128)(2,1)}, bf16[1,256,256]{1,2,0:T(8,128)(2,1)S(1)}, u32[]{:S(2)}) copy-start(bf16[1,256,256]{1,2,0:T(8,128)(2,1)S(1)} %copy.302) | copy-start | bytes 393220
  64.0 16.1 %all-to-all-start.4 = ((bf16[64,4,2,512]{3,2,0,1:T(2,128)(2,1)}), bf16[64,4,2,512]{3,2,0,1:T(2,128)(2,1)S(1)}, u32[]{:S(2)}, u32[]{:S(2)}) async-start(bf16[64,4,2,512]{3,2,0,1:T(2,128)(2,1)} %copy.325), calls=%async_computation.4 | async-start | bytes 1048576 | tf_op jit(solution)/shard_map/all_to_all | solution.py:41
  67.9 1.5 copy-start.6
  70.2 6.9 %copy-start = (f32[2,2,256,256]{2,3,1,0:T(8,128)}, f32[2,2,256,256]{2,3,1,0:T(8,128)S(1)}, u32[]{:S(2)}) copy-start(f32[2,2,256,256]{2,3,1,0:T(8,128)S(1)} %get-tuple-element.80) | copy-start | bytes 3145732
  70.2 6.3 %copy-start.42 = (f32[2,2,256]{2,1,0:T(2,128)}, f32[2,2,256]{2,1,0:T(2,128)S(1)}, u32[]{:S(2)}) copy-start(f32[2,2,256]{2,1,0:T(2,128)S(1)} %get-tuple-element.17) | copy-start | bytes 12292
  70.2 6.3 %copy-start.44 = (f32[2,2,256]{2,1,0:T(2,128)}, f32[2,2,256]{2,1,0:T(2,128)S(1)}, u32[]{:S(2)}) copy-start(f32[2,2,256]{2,1,0:T(2,128)S(1)} %get-tuple-element.18) | copy-start | bytes 12292
  70.7 1.9 copy-start.37
  72.7 1.9 copy-start.36
  81.0 1.3 copy-start.17
  81.0 1.3 copy-start.31
  82.3 1.4 copy-start.21
  82.3 1.4 copy-start.29
  88.1 1.5 copy-start.2
  88.1 1.5 copy-start.4
  88.1 1.5 copy-start.34
  89.6 1.2 copy-start.3
  89.6 1.2 copy-start.33
  90.9 3.1 %copy-start.11 = (f32[2,2,256,256]{2,3,1,0:T(8,128)S(1)}, f32[2,2,256,256]{2,3,1,0:T(8,128)}, u32[]{:S(2)}) copy-start(f32[2,2,256,256]{2,3,1,0:T(8,128)} %get-tuple-element.82) | copy-start | bytes 3145732
  90.9 3.1 %copy-start.12 = (f32[2,2,256,256]{2,3,1,0:T(8,128)S(1)}, f32[2,2,256,256]{2,3,1,0:T(8,128)}, u32[]{:S(2)}) copy-start(f32[2,2,256,256]{2,3,1,0:T(8,128)} %get-tuple-element.81) | copy-start | bytes 3145732
  91.3 2.7 %copy-start.10 = (f32[2,2,256,256]{2,3,1,0:T(8,128)S(1)}, f32[2,2,256,256]{2,3,1,0:T(8,128)}, u32[]{:S(2)}) copy-start(f32[2,2,256,256]{2,3,1,0:T(8,128)} %get-tuple-element.83) | copy-start | bytes 3145732
  92.3 1.7 copy-start.1
  94.0 1.4 copy-start.7
  103.1 6.1 %copy-start.9 = (bf16[2,2,256,256]{2,3,1,0:T(8,128)(2,1)S(1)}, bf16[2,2,256,256]{2,3,1,0:T(8,128)(2,1)}, u32[]{:S(2)}) copy-start(bf16[2,2,256,256]{2,3,1,0:T(8,128)(2,1)} %get-tuple-element.57) | copy-start | bytes 1572868
  105.0 4.3 %copy-start.8 = (bf16[256,1,1,512]{0,3,2,1:T(8,128)(2,1)S(1)}, bf16[256,1,1,512]{0,3,2,1:T(8,128)(2,1)}, u32[]{:S(2)}) copy-start(bf16[256,1,1,512]{0,3,2,1:T(8,128)(2,1)} %copy-done.6) | copy-start | bytes 786436
  107.3 80.8 %collective-permute-start.4 = (bf16[2,256,256]{2,0,1:T(2,128)(2,1)}, bf16[2,256,256]{2,0,1:T(2,128)(2,1)}, u32[]{:S(2)}, u32[]{:S(2)}) collective-permute-start(bf16[2,256,256]{2,0,1:T(2,128)(2,1)} %pad_maximum_fusion.8), channel_id=1, source_target_pairs={{4,0},{8,4},{12,8},{16,12},{20,16},{24,20},{28,24},{32,28},{36,32}... | collective-permute-start | bytes 786440 | tf_op jit(solution)/shard_map/ppermute | solution.py:19
  116.0 72.1 %collective-permute-start.5 = (bf16[2,256,256]{2,0,1:T(2,128)(2,1)}, bf16[2,256,256]{2,0,1:T(2,128)(2,1)}, u32[]{:S(2)}, u32[]{:S(2)}) collective-permute-start(bf16[2,256,256]{2,0,1:T(2,128)(2,1)} %pad_maximum_fusion.9), channel_id=1, source_target_pairs={{8,0},{12,4},{16,8},{20,12},{24,16},{28,20},{32,24},{36,28},{40,32... | collective-permute-start | bytes 786440 | tf_op jit(solution)/shard_map/ppermute | solution.py:19
  130.1 67.3 %collective-permute-start.6 = (bf16[2,256,256]{2,0,1:T(2,128)(2,1)}, bf16[2,256,256]{2,0,1:T(2,128)(2,1)}, u32[]{:S(2)}, u32[]{:S(2)}) collective-permute-start(bf16[2,256,256]{2,0,1:T(2,128)(2,1)} %pad_maximum_fusion.10), channel_id=1, source_target_pairs={{4,0},{8,4},{12,8},{16,12},{20,16},{24,20},{28,24},{32,28},{36,32}... | collective-permute-start | bytes 786440 | tf_op jit(solution)/shard_map/ppermute | solution.py:19
  136.5 28.3 %copy-start.14 = (f32[2,128,2,256]{3,1,2,0:T(8,128)S(1)}, f32[2,128,2,256]{3,1,2,0:T(8,128)}, u32[]{:S(2)}) copy-start(f32[2,128,2,256]{3,1,2,0:T(8,128)} %fusion.92) | copy-start | bytes 1572868
  136.5 28.3 %copy-start.24 = (bf16[1,256,256]{1,2,0:T(8,128)(2,1)S(1)}, bf16[1,256,256]{1,2,0:T(8,128)(2,1)}, u32[]{:S(2)}) copy-start(bf16[1,256,256]{1,2,0:T(8,128)(2,1)} %copy.293) | copy-start | bytes 393220
  138.9 58.6 %collective-permute-start.7 = (bf16[2,256,256]{2,0,1:T(2,128)(2,1)}, bf16[2,256,256]{2,0,1:T(2,128)(2,1)}, u32[]{:S(2)}, u32[]{:S(2)}) collective-permute-start(bf16[2,256,256]{2,0,1:T(2,128)(2,1)} %pad_maximum_fusion.11), channel_id=1, source_target_pairs={{8,0},{12,4},{16,8},{20,12},{24,16},{28,20},{32,24},{36,28},{40,32... | collective-permute-start | bytes 786440 | tf_op jit(solution)/shard_map/ppermute | solution.py:19
  166.4 17.8 %all-to-all-start.2 = ((bf16[4,64,1,512]{3,1,2,0:T(8,128)(2,1)}), bf16[4,64,1,512]{3,1,2,0:T(8,128)(2,1)S(1)}, u32[]{:S(2)}, u32[]{:S(2)}) async-start(bf16[4,64,1,512]{3,1,2,0:T(8,128)(2,1)} %pad_maximum_fusion.5), calls=%async_computation.2 | async-start | bytes 524288 | tf_op jit(solution)/shard_map/all_to_all | solution.py:121
  170.0 1.1 copy-start.22
  172.6 14.9 %copy-start.5 = (bf16[256,1,1,512]{0,3,2,1:T(8,128)(2,1)S(1)}, bf16[256,1,1,512]{0,3,2,1:T(8,128)(2,1)}, u32[]{:S(2)}) copy-start(bf16[256,1,1,512]{0,3,2,1:T(8,128)(2,1)} %copy.337) | copy-start | bytes 786436
  184.1 9.4 %all-to-all-start.5 = ((bf16[4,64,1,512]{3,1,2,0:T(8,128)(2,1)}), bf16[4,64,1,512]{3,1,2,0:T(8,128)(2,1)S(1)}, u32[]{:S(2)}, u32[]{:S(2)}) async-start(bf16[4,64,1,512]{3,1,2,0:T(8,128)(2,1)} %pad_maximum_fusion.7), calls=%async_computation.5 | async-start | bytes 524288 | tf_op jit(solution)/shard_map/all_to_all | solution.py:121
  193.5 9.4 %all-to-all-start.6 = ((bf16[256,1,2,256]{3,2,1,0:T(2,128)(2,1)}), bf16[256,1,2,256]{3,2,1,0:T(2,128)(2,1)S(1)}, u32[]{:S(2)}, u32[]{:S(2)}) async-start(bf16[256,1,2,256]{3,2,1,0:T(2,128)(2,1)} %fusion.69), calls=%async_computation.6 | async-start | bytes 524288 | tf_op jit(solution)/shard_map/all_to_all | solution.py:132
  202.9 9.4 %all-to-all-start.7 = ((bf16[256,1,2,256]{3,2,1,0:T(2,128)(2,1)}), bf16[256,1,2,256]{3,2,1,0:T(2,128)(2,1)S(1)}, u32[]{:S(2)}, u32[]{:S(2)}) async-start(bf16[256,1,2,256]{3,2,1,0:T(2,128)(2,1)} %fusion.68), calls=%async_computation.7 | async-start | bytes 524288 | tf_op jit(solution)/shard_map/all_to_all | solution.py:132
  (20 other events, 18.6 us)
